TPU v7x, 256 devices: a whole 4x4x8 slice. The times are simulated.
256 devices in a mesh: seq: 32 (over x, z), tensor: 8 (over y, core).
Axes of the slice: x: 4, y: 4, z: 8, core: 2. Of those that a mesh axis runs over, the one named last changes fastest.
Arguments:
- queries: bfloat16 [10240, 4096], P('seq', 'tensor'), may hold values from -8 to 8
- key_rows: bfloat16 [10240, 1024], P('seq', 'tensor'), may hold values from -8 to 8
- value_rows: bfloat16 [10240, 1024], P('seq', 'tensor'), may hold values from -6 to 6
- out_weight: bfloat16 [4096, 8192], P('tensor', 'seq'), may hold values from -0.09375 to 0.09375
- residual_in: bfloat16 [10240, 8192], P('seq'), may hold values from -0.1796875 to 0.1796875
- norm_gain: bfloat16 [8192], replicated, may hold values from 0.099609375 to 1.8984375
- prompt_lengths: int32 [18], replicated, may hold values from 1 to 5120, 10240 in all
Outputs:
- normed: bfloat16 [10240, 8192], P('seq')
- cache_keys: bfloat16 [22528, 1024], P('seq', 'tensor')
- cache_values: bfloat16 [22528, 1024], P('seq', 'tensor')
Inputs may be any that keep to these rules, and one draw needn't show every extreme that they name: `prompt_lengths`: the 18 lengths sum to 10240, and the largest is 5120.
All inputs are finite; a program needn't handle non-finite values.
Results may differ from a plain program's by a relative error of at most 0.019.
Values may be sent and summed in bfloat16 or wider, within the bound.
No kernel may reach another device: no remote copies, remote signals or barrier semaphores. Data moves between devices by JAX's collectives and lax.ppermute only.
A program may use at most 192 MiB of HBM per device.

v0:
```python
import math
import jax
import jax.numpy as jnp
from jax import lax
from jax.sharding import PartitionSpec as P

HD = 128
PAGE = 128
SLOT_DEV = 704


def position_of(stored, per_device, devices):
    half_block = per_device // 2
    device = stored // per_device
    offset = stored % per_device
    return jnp.where(
        offset < half_block,
        device * half_block + offset,
        (2 * devices - 1 - device) * half_block + offset - half_block,
    )


def stored_row(position, per_device, devices):
    half_block = per_device // 2
    block_index = position // half_block
    device = jnp.where(block_index < devices, block_index, 2 * devices - 1 - block_index)
    offset = position % half_block + jnp.where(block_index < devices, 0, half_block)
    return device * per_device + offset


def segment_of(position, lengths):
    doc_ends = jnp.cumsum(lengths, dtype=jnp.int32)
    return jnp.sum(
        (position[:, None] >= doc_ends[None, :]).astype(jnp.int32), axis=1, dtype=jnp.int32
    )


def slot_source(slot_ids, lengths, page_size):
    padded = (lengths + page_size - 1) // page_size * page_size
    page_ends = jnp.cumsum(padded, dtype=jnp.int32)
    page_starts = page_ends - padded
    doc_ends = jnp.cumsum(lengths, dtype=jnp.int32)
    doc_starts = doc_ends - lengths
    before = (slot_ids[:, None] >= page_ends[None, :]).astype(jnp.int32)
    inside = (slot_ids[:, None] >= page_starts[None, :]).astype(jnp.int32) - before
    page_start = jnp.sum(before * padded[None, :], axis=1, dtype=jnp.int32)
    doc_start = jnp.sum(before * lengths[None, :], axis=1, dtype=jnp.int32)
    length = jnp.sum(inside * lengths[None, :], axis=1, dtype=jnp.int32)
    within = slot_ids - page_start
    is_live = within < length
    return (doc_start + within, is_live)


def body(queries, key_rows, value_rows, out_weight, residual_in, norm_gain, prompt_lengths):
    seq_count = lax.axis_size("seq")
    seq_index = lax.axis_index("seq")
    per_device = queries.shape[0]
    kv_local = key_rows.shape[1] // HD
    group_size = queries.shape[1] // (kv_local * HD)
    score_scale = 1.0 / math.sqrt(HD)
    local_rows = jnp.arange(per_device, dtype=jnp.int32) + seq_index * per_device
    my_position = position_of(local_rows, per_device, seq_count)
    my_segment = segment_of(my_position, prompt_lengths)
    grouped = queries.reshape(per_device, kv_local, group_size, HD)
    kv_width = key_rows.shape[1]
    kv_piece = lax.all_gather(
        jnp.concatenate([key_rows, value_rows], axis=1), "seq", axis=0, tiled=True
    )
    key_piece = kv_piece[:, :kv_width]
    value_piece = kv_piece[:, kv_width:]
    piece_rows = key_piece.shape[0]
    key_position = position_of(jnp.arange(piece_rows, dtype=jnp.int32), per_device, seq_count)
    key_segment = segment_of(key_position, prompt_lengths)
    allowed = (key_position[None, :] <= my_position[:, None]) & (
        key_segment[None, :] == my_segment[:, None]
    )
    top_old = jnp.full((kv_local, group_size, per_device), -1e30, jnp.float32)
    scores = (
        jnp.einsum(
            "qgjd,kgd->gjqk",
            grouped,
            key_piece.reshape(piece_rows, kv_local, HD),
            preferred_element_type=jnp.float32,
        )
        * score_scale
    )
    scores = jnp.where(allowed, scores, -1e30)
    top_new = jnp.maximum(top_old, jnp.max(scores, axis=-1))
    weights = jnp.where(allowed, jnp.exp(scores - top_new[..., None]), 0.0)
    total_new = jnp.sum(weights, axis=-1)
    accum_new = jnp.einsum(
        "gjqk,kgd->gjqd",
        weights.astype(jnp.bfloat16),
        value_piece.reshape(piece_rows, kv_local, HD),
        preferred_element_type=jnp.float32,
    )
    attended = jnp.transpose(accum_new / total_new[..., None], (2, 0, 1, 3))
    attended = attended.reshape(per_device, -1).astype(jnp.bfloat16)
    partial_value = jnp.dot(
        attended,
        lax.all_gather(out_weight, "seq", axis=1, tiled=True),
        preferred_element_type=jnp.float32,
    )
    projected = lax.psum(partial_value.astype(jnp.bfloat16), "tensor").astype(jnp.float32)
    hidden = residual_in.astype(jnp.float32) + projected
    mean_square = jnp.mean(hidden * hidden, axis=-1, keepdims=True)
    normed = (hidden * lax.rsqrt(mean_square + 1e-05) * norm_gain.astype(jnp.float32)).astype(
        jnp.bfloat16
    )
    slot_ids = seq_index * SLOT_DEV + jnp.arange(SLOT_DEV, dtype=jnp.int32)
    source, is_live = slot_source(slot_ids, prompt_lengths, PAGE)
    target = stored_row(source, per_device, seq_count)
    empty_cache = jnp.zeros((SLOT_DEV, kv_local * HD), jnp.bfloat16)
    found = is_live & (target >= 0) & (target < piece_rows)
    safe_index = jnp.clip(target, 0, piece_rows - 1)
    cache_keys = jnp.where(found[:, None], jnp.take(key_piece, safe_index, axis=0), empty_cache)
    cache_values = jnp.where(found[:, None], jnp.take(value_piece, safe_index, axis=0), empty_cache)
    return (normed, cache_keys, cache_values)


def solution(mesh):
    return jax.shard_map(
        body,
        mesh=mesh,
        in_specs=(
            P("seq", "tensor"),
            P("seq", "tensor"),
            P("seq", "tensor"),
            P("tensor", "seq"),
            P("seq", None),
            P(),
            P(),
        ),
        out_specs=(P("seq", None), P("seq", "tensor"), P("seq", "tensor")),
        check_vma=False,
    )
```

profile of v0, /device:TPU:1, one launch (start us, length us, event | category | flops | bytes accessed | tf_op | source)
XLA Modules:
  0.0 310.1 jit_solution(13555092218789178911)
XLA Ops:
  7.2 0.0 copy-start
  7.2 0.0 all-gather.3.cloned.1.call-start
  7.2 1.6 pad_maximum_fusion
  8.9 0.0 all-gather.3.cloned.1.call-update
  8.9 0.0 all-gather.5.cloned.1.call-start
  9.0 0.7 all-gather.5.cloned.1.call-update
  9.7 0.0 all-reduce.2.cloned.1.call-start
  9.7 0.7 copy.17
  10.5 0.1 reduce.2
  10.6 0.7 convert_element_type.52
  11.3 0.7 fusion.65
  12.0 0.1 copy.20
  12.1 0.1 reduce.3
  12.3 0.7 fusion.55
  13.0 0.7 fusion.64
  13.6 0.8 fusion.36
  14.5 0.1 convert_reduce_fusion.1
  14.6 0.2 convert_reduce_fusion
  14.8 4.6 %compare_and_fusion = pred[320,10240]{1,0:T(8,128)(4,1)} fusion(s32[10240]{0:T(1024)S(1)} %convert_reduce_fusion, s32[10240]{0:T(1024)S(1)} %fusion.43, s32[320]{0:T(512)S(1)} %convert_reduce_fusion.1, s32[320]{0:T(512)S(1)} %add_select_fusion.5), kind=kLoop, calls=%fused_computation.10 | loop fusion | flops 9830400 | bytes 3361280 | tf_op jit(solution)/shard_map/and | solution.py:74
  19.4 78.3 %all-gather.3.cloned.1.call-done = bf16[10240,256]{1,0:T(8,128)(2,1)} async-done(((bf16[320,256]{1,0:T(8,128)(2,1)}), bf16[10240,256]{1,0:T(8,128)(2,1)}) %all-gather.3.cloned.1.call-update) | async-done | bytes 5242896 | tf_op jit(solution)/shard_map/all_gather | solution.py:66
  97.7 0.0 copy-done
  97.7 22.9 %fusion = (f32[4,320]{1,0:T(4,128)S(1)}, f32[10240,320,4]{0,1,2:T(8,128)}) fusion(pred[320,10240]{1,0:T(8,128)(4,1)} %compare_and_fusion, bf16[10240,256]{1,0:T(8,128)(2,1)} %all-gather.3.cloned.1.call-done, bf16[320,512]{1,0:T(8,128)(2,1)S(1)} %copy-done), kind=kOutput, calls=%fused_computation.4 | convolution fusion | flops 3394763520 | bytes 58659840 | tf_op jit(solution)/shard_map/qgjd,kgd->gjqk/dot_general | solution.py:79
  120.5 22.7 %fusion.1 = f32[4,320]{1,0:T(4,128)S(1)} fusion(f32[10240,320,4]{0,1,2:T(8,128)} %get-tuple-element.14, f32[4,320]{1,0:T(4,128)S(1)} %broadcast_maximum_fusion, pred[320,10240]{1,0:T(8,128)(4,1)} %compare_and_fusion), kind=kLoop, calls=%fused_computation.5 | loop fusion | flops 65534720 | bytes 55715840 | tf_op jit(solution)/shard_map/reduce_sum | solution.py:90
  143.3 23.2 %fusion.20 = bf16[320,1,4,128]{3,0,2,1:T(8,128)(2,1)S(1)} fusion(f32[10240,320,4]{0,1,2:T(8,128)} %get-tuple-element.14, f32[4,320]{1,0:T(4,128)S(1)} %broadcast_maximum_fusion, pred[320,10240]{1,0:T(8,128)(4,1)} %compare_and_fusion, f32[4,320]{1,0:T(4,128)S(1)} %fusion.1, bf16[10240,256]{1,0:T(8,128)(2,1)} %all-gather.3.cloned.1.call-done), kind=kOutput, calls=%fused_computation.20 | convolution fusion | flops 3421306880 | bytes 58664960 | tf_op jit(solution)/shard_map/gjqk,kgd->gjqd/dot_general | solution.py:91
  166.5 0.3 copy.19
  166.8 34.2 %all-gather.5.cloned.1.call-done = bf16[512,8192]{1,0:T(8,128)(2,1)} async-done(((bf16[512,256]{1,0:T(8,128)(2,1)}), bf16[512,8192]{1,0:T(8,128)(2,1)}) %all-gather.5.cloned.1.call-update) | async-done | bytes 8388624 | tf_op jit(solution)/shard_map/all_gather | solution.py:101
  200.9 8.0 %convolution_convert_fusion = bf16[320,8192]{1,0:T(8,128)(2,1)} fusion(bf16[512,8192]{1,0:T(8,128)(2,1)} %all-gather.5.cloned.1.call-done, bf16[40,8,4,128]{3,2,1,0:T(4,128)(2,1)S(1)} %bitcast.67), kind=kOutput, calls=%fused_computation.11 | convolution fusion | flops 2686976000 | bytes 13959168 | tf_op jit(solution)/shard_map/dot_general | solution.py:99
  208.9 0.0 all-reduce.2.cloned.1.call-update
  208.9 3.7 %fusion.62 = (bf16[10240,128]{1,0:T(8,128)(2,1)S(1)}, bf16[10240,128]{1,0:T(8,128)(2,1)}) fusion(bf16[10240,256]{1,0:T(8,128)(2,1)} %all-gather.3.cloned.1.call-done), kind=kLoop, calls=%fused_computation.91 | loop fusion | bytes 10485760 | tf_op jit(solution)/shard_map/slice | solution.py:70
  212.6 3.8 %gather_fusion = bf16[704,128]{1,0:T(8,128)(2,1)S(1)} fusion(bf16[10240,128]{1,0:T(8,128)(2,1)} %get-tuple-element.10, s32[1024]{0:T(1024)S(1)} %pad_clamp_fusion), kind=kCustom, calls=%fused_computation.clone | custom fusion | bytes 363264 | tf_op jit(solution)/shard_map/jit(_take)/gather | solution.py:116
  216.5 2.0 gather_fusion.1
  218.5 1.0 select_select_fusion
  219.5 71.0 %all-reduce.2.cloned.1.call-done = bf16[320,8192]{1,0:T(8,128)(2,1)} async-done(((bf16[320,8192]{1,0:T(8,128)(2,1)}), bf16[320,8192]{1,0:T(8,128)(2,1)}) %all-reduce.2.cloned.1.call-update) | async-done | bytes 5242896 | tf_op jit(solution)/shard_map/psum | solution.py:104
  290.5 0.0 copy-start.2
  290.5 0.0 copy-start.1
  290.5 6.0 %multiply_reduce_fusion = f32[320]{0:T(512)S(1)} fusion(bf16[320,8192]{1,0:T(8,128)(2,1)} %all-reduce.2.cloned.1.call-done, bf16[320,8192]{1,0:T(8,128)(2,1)} %param.13), kind=kLoop, calls=%fused_computation.13 | loop fusion | flops 13106880 | bytes 10487040 | tf_op jit(solution)/shard_map/reduce_sum | solution.py:106
  296.5 0.0 copy-done.2
  296.5 7.1 %multiply_convert_fusion = bf16[320,8192]{1,0:T(8,128)(2,1)} fusion(bf16[320,8192]{1,0:T(8,128)(2,1)S(1)} %copy-done.2, bf16[320,8192]{1,0:T(8,128)(2,1)} %param.13, f32[8192]{0:T(1024)S(1)} %convert_element_type.52, f32[320]{0:T(512)S(1)} %add_rsqrt_fusion), kind=kLoop, calls=%fused_computation.12 | loop fusion | flops 15728640 | bytes 15762688 | tf_op jit(solution)/shard_map/convert_element_type | solution.py:107
  303.6 0.0 copy-done.1
  (11 shorter events, 0.2 us)
Async XLA Ops:
  7.2 90.5 %copy-start = (bf16[320,512]{1,0:T(8,128)(2,1)S(1)}, bf16[320,512]{1,0:T(8,128)(2,1)}, u32[]{:S(2)}) copy-start(bf16[320,512]{1,0:T(8,128)(2,1)} %param.9) | copy-start | bytes 983044
  7.2 90.5 %all-gather.3.cloned.1.call-start = ((), (), s32[]{:S(2)}) async-start(), calls=%async_computation | async-start | bytes 5406720 | tf_op jit(solution)/shard_map/all_gather | solution.py:66
  8.9 192.0 %all-gather.5.cloned.1.call-start = ((), (), s32[]{:S(2)}) async-start(), calls=%async_computation.1 | async-start | bytes 8650752 | tf_op jit(solution)/shard_map/all_gather | solution.py:101
  9.7 280.8 %all-reduce.2.cloned.1.call-start = ((), (), s32[]{:S(2)}) async-start(), calls=%async_computation.2 | async-start | bytes 10485760 | tf_op jit(solution)/shard_map/psum | solution.py:104
  290.5 6.0 %copy-start.2 = (bf16[320,8192]{1,0:T(8,128)(2,1)S(1)}, bf16[320,8192]{1,0:T(8,128)(2,1)}, u32[]{:S(2)}) copy-start(bf16[320,8192]{1,0:T(8,128)(2,1)} %all-reduce.2.cloned.1.call-done) | copy-start | bytes 15728644
  290.5 13.1 %copy-start.1 = (bf16[320,512]{1,0:T(8,128)(2,1)S(1)}, bf16[320,512]{1,0:T(8,128)(2,1)}, u32[]{:S(2)}) copy-start(bf16[320,512]{1,0:T(8,128)(2,1)} %param.9) | copy-start | bytes 983044
Sparse Core Ops, SparseCore 0:
  11.2 86.4 all-gather.2
  100.1 100.7 all-gather.4
  209.0 81.3 all-reduce.1
where the time goes:
time: 310 us
  waiting for transfers between devices  184 us (59%)
  matrix products  54.1 us (17%)
  other arithmetic  47.3 us (15%)
  between operations  13.9 us (4%)
  local copies, waits for them, and re-layouts  10.7 us (3%)
    all_gather x1, waiting for transfers between devices, body(): lax.all_gather(jnp.concatenate([key_rows, value_rows], axis=1), 'seq', ax...  78.3 us
    psum x1, waiting for transfers between devices, body(): lax.psum(partial_value.astype(jnp.bfloat16), 'tensor').astype(jnp.float32)  71 us
    all_gather x1, waiting for transfers between devices, body(): lax.all_gather(out_weight, 'seq', axis=1, tiled=True)  34.2 us
    dot_general x1, matrix products, body(): jnp.einsum('gjqk,kgd->gjqd', weights.astype(jnp.bfloat16), value_piece.re...  23.2 us
    dot_general x1, matrix products, body(): jnp.einsum('qgjd,kgd->gjqk', grouped, key_piece.reshape(piece_rows, kv_lo...  22.9 us
    reduce_sum x1, other arithmetic, body(): total_new = jnp.sum(weights, axis=-1)  22.7 us
    dot_general x1, matrix products, body(): jnp.dot(attended, lax.all_gather(out_weight, 'seq', axis=1, tiled=True),...  7.96 us
    convert_element_type x1, other arithmetic, body(): (hidden * lax.rsqrt(mean_square + 1e-05) * norm_gain.astype(jnp.float32))...  7.13 us
  transfers between devices with their start and end apart: 3, of which 3 were waited for; matrix products, arithmetic and copies ran while one was open for 29% of the time, Pallas kernels for 0%

commit v1 on v0

--- a/solution.py
+++ b/solution.py
@@ -63,9 +63,9 @@
     my_segment = segment_of(my_position, prompt_lengths)
     grouped = queries.reshape(per_device, kv_local, group_size, HD)
     kv_width = key_rows.shape[1]
-    kv_piece = lax.all_gather(
-        jnp.concatenate([key_rows, value_rows], axis=1), "seq", axis=0, tiled=True
-    )
+    part = jnp.concatenate([key_rows, value_rows], axis=1)
+    outgoing = jnp.stack([part] * lax.axis_size("seq"))
+    kv_piece = jnp.concatenate(lax.all_to_all(outgoing, "seq", 0, 0), axis=0)
     key_piece = kv_piece[:, :kv_width]
     value_piece = kv_piece[:, kv_width:]
     piece_rows = key_piece.shape[0]

time: 310 us -> 339 us (1.094)
  waiting for transfers between devices: 184 us -> 202 us
  starting transfers between devices: 0.12 us -> 12.1 us
  other arithmetic: 47.3 us -> 43.3 us
    all_to_all x0 -> x1, waiting for transfers between devices: none -> 123 us  [body(): kv_piece = jnp.concatenate(lax.all_to_all(outgoing, 'seq', 0, 0), axis=0)]
    all_gather x1 -> x0, waiting for transfers between devices: 78.3 us -> none  [body(): lax.all_gather(jnp.concatenate([key_rows, value_rows], axis=1), 'seq', ax...]
    all_gather x1, waiting for transfers between devices: 34.2 us -> 0.02 us  [body(): lax.all_gather(out_weight, 'seq', axis=1, tiled=True)]
    all_to_all x0 -> x1, starting transfers between devices: none -> 12 us  [body(): kv_piece = jnp.concatenate(lax.all_to_all(outgoing, 'seq', 0, 0), axis=0)]
    psum x1, waiting for transfers between devices: 71 us -> 77.8 us  [body(): lax.psum(partial_value.astype(jnp.bfloat16), 'tensor').astype(jnp.float32)]
  transfers between devices with their start and end apart: 3 -> 3, of which waited for: 3 -> 2; matrix products, arithmetic and copies ran while one was open for 29% -> 25% of each run, Pallas kernels for 0% -> 0%
where the time goes in v1:
time: 339 us
  waiting for transfers between devices  202 us (60%)
  matrix products  54.7 us (16%)
  other arithmetic  43.3 us (13%)
  between operations  14.2 us (4%)
  local copies, waits for them, and re-layouts  13 us (4%)
  starting transfers between devices  12.1 us (4%)
    all_to_all x1, waiting for transfers between devices, body(): kv_piece = jnp.concatenate(lax.all_to_all(outgoing, 'seq', 0, 0), axis=0)  123 us
    psum x1, waiting for transfers between devices, body(): lax.psum(partial_value.astype(jnp.bfloat16), 'tensor').astype(jnp.float32)  77.8 us
    dot_general x1, matrix products, body(): jnp.einsum('qgjd,kgd->gjqk', grouped, key_piece.reshape(piece_rows, kv_lo...  23.4 us
    dot_general x1, matrix products, body(): jnp.einsum('gjqk,kgd->gjqd', weights.astype(jnp.bfloat16), value_piece.re...  23.1 us
    reduce_sum x1, other arithmetic, body(): total_new = jnp.sum(weights, axis=-1)  22.8 us
    all_to_all x1, starting transfers between devices, body(): kv_piece = jnp.concatenate(lax.all_to_all(outgoing, 'seq', 0, 0), axis=0)  12 us
    dot_general x1, matrix products, body(): jnp.dot(attended, lax.all_gather(out_weight, 'seq', axis=1, tiled=True),...  8.21 us
    convert_element_type x1, other arithmetic, body(): (hidden * lax.rsqrt(mean_square + 1e-05) * norm_gain.astype(jnp.float32))...  7.13 us
  transfers between devices with their start and end apart: 3, of which 2 were waited for; matrix products, arithmetic and copies ran while one was open for 25% of the time, Pallas kernels for 0%

profile of v1, /device:TPU:1, one launch (start us, length us, event | category | flops | bytes accessed | tf_op | source)
XLA Modules:
  0.0 339.1 jit_solution(2640158884365046821)
XLA Ops:
  7.2 0.0 copy-start
  7.2 0.0 copy-start.4
  7.2 0.0 copy-start.3
  7.2 1.0 pad_maximum_fusion
  8.2 2.9 stack.2
  11.1 12.0 %all-to-all-start = ((bf16[32,320,256]{2,1,0:T(8,128)(2,1)}), bf16[32,320,256]{2,1,0:T(8,128)(2,1)}, u32[]{:S(2)}, u32[]{:S(2)}) async-start(bf16[32,320,256]{2,1,0:T(8,128)(2,1)} %stack.2), calls=%async_computation | async-start | bytes 10485760 | tf_op jit(solution)/shard_map/all_to_all | solution.py:68
  23.1 0.0 all-gather.2.cloned.1.call-start
  23.2 0.7 all-gather.2.cloned.1.call-update
  23.9 0.0 all-reduce.2.cloned.1.call-start
  23.9 0.0 copy-done.4
  23.9 0.1 copy.17
  24.1 0.1 reduce.2
  24.2 0.0 copy-done.3
  24.2 0.1 copy.20
  24.4 0.1 reduce.3
  24.5 0.1 fusion.36
  24.7 0.1 convert_reduce_fusion.1
  24.9 0.2 convert_reduce_fusion
  25.1 4.5 %compare_and_fusion = pred[320,10240]{1,0:T(8,128)(4,1)} fusion(s32[10240]{0:T(1024)S(1)} %convert_reduce_fusion, s32[10240]{0:T(1024)S(1)} %fusion.43, s32[320]{0:T(512)S(1)} %convert_reduce_fusion.1, s32[320]{0:T(512)S(1)} %add_select_fusion.5), kind=kLoop, calls=%fused_computation.10 | loop fusion | flops 9830400 | bytes 3361280 | tf_op jit(solution)/shard_map/and | solution.py:74
  29.7 123.2 %all-to-all-done = bf16[32,320,256]{2,1,0:T(8,128)(2,1)} async-done(((bf16[32,320,256]{2,1,0:T(8,128)(2,1)}), bf16[32,320,256]{2,1,0:T(8,128)(2,1)}, u32[]{:S(2)}, u32[]{:S(2)}) %all-to-all-start) | async-done | bytes 5242912 | tf_op jit(solution)/shard_map/all_to_all | solution.py:68
  152.9 0.0 copy-done
  152.9 23.4 %fusion = (f32[4,320]{1,0:T(4,128)S(1)}, f32[10240,320,4]{0,1,2:T(8,128)}) fusion(pred[320,10240]{1,0:T(8,128)(4,1)} %compare_and_fusion, bf16[10240,256]{1,0:T(8,128)(2,1)} %bitcast.1, bf16[320,512]{1,0:T(8,128)(2,1)S(1)} %copy-done), kind=kOutput, calls=%fused_computation.4 | convolution fusion | flops 3394763520 | bytes 58659840 | tf_op jit(solution)/shard_map/qgjd,kgd->gjqk/dot_general | solution.py:79
  176.3 22.8 %fusion.1 = f32[4,320]{1,0:T(4,128)S(1)} fusion(f32[10240,320,4]{0,1,2:T(8,128)} %get-tuple-element.14, f32[4,320]{1,0:T(4,128)S(1)} %broadcast_maximum_fusion, pred[320,10240]{1,0:T(8,128)(4,1)} %compare_and_fusion), kind=kLoop, calls=%fused_computation.5 | loop fusion | flops 65534720 | bytes 55715840 | tf_op jit(solution)/shard_map/reduce_sum | solution.py:90
  199.1 23.1 %fusion.20 = bf16[320,1,4,128]{3,0,2,1:T(8,128)(2,1)S(1)} fusion(f32[10240,320,4]{0,1,2:T(8,128)} %get-tuple-element.14, f32[4,320]{1,0:T(4,128)S(1)} %broadcast_maximum_fusion, pred[320,10240]{1,0:T(8,128)(4,1)} %compare_and_fusion, f32[4,320]{1,0:T(4,128)S(1)} %fusion.1, bf16[10240,256]{1,0:T(8,128)(2,1)} %bitcast.1), kind=kOutput, calls=%fused_computation.20 | convolution fusion | flops 3421306880 | bytes 58664960 | tf_op jit(solution)/shard_map/gjqk,kgd->gjqd/dot_general | solution.py:91
  222.2 0.3 copy.19
  222.5 0.0 all-gather.2.cloned.1.call-done
  222.5 8.2 %convolution_convert_fusion = bf16[320,8192]{1,0:T(8,128)(2,1)} fusion(bf16[512,8192]{1,0:T(8,128)(2,1)} %all-gather.2.cloned.1.call-done, bf16[40,8,4,128]{3,2,1,0:T(4,128)(2,1)S(1)} %bitcast.68), kind=kOutput, calls=%fused_computation.11 | convolution fusion | flops 2686976000 | bytes 13959168 | tf_op jit(solution)/shard_map/dot_general | solution.py:99
  230.7 0.0 all-reduce.2.cloned.1.call-update
  230.7 3.7 %fusion.62 = (bf16[10240,128]{1,0:T(8,128)(2,1)S(1)}, bf16[10240,128]{1,0:T(8,128)(2,1)}) fusion(bf16[10240,256]{1,0:T(8,128)(2,1)} %bitcast.1), kind=kLoop, calls=%fused_computation.91 | loop fusion | bytes 10485760 | tf_op jit(solution)/shard_map/slice | solution.py:70
  234.5 3.8 %gather_fusion = bf16[704,128]{1,0:T(8,128)(2,1)S(1)} fusion(bf16[10240,128]{1,0:T(8,128)(2,1)} %get-tuple-element.10, s32[1024]{0:T(1024)S(1)} %pad_clamp_fusion), kind=kCustom, calls=%fused_computation.clone | custom fusion | bytes 363264 | tf_op jit(solution)/shard_map/jit(_take)/gather | solution.py:116
  238.3 2.0 gather_fusion.1
  240.3 1.0 select_select_fusion
  241.3 77.8 %all-reduce.2.cloned.1.call-done = bf16[320,8192]{1,0:T(8,128)(2,1)} async-done(((bf16[320,8192]{1,0:T(8,128)(2,1)}), bf16[320,8192]{1,0:T(8,128)(2,1)}) %all-reduce.2.cloned.1.call-update) | async-done | bytes 5242896 | tf_op jit(solution)/shard_map/psum | solution.py:104
  319.1 0.0 copy-start.2
  319.1 0.0 copy-start.1
  319.1 6.0 %multiply_reduce_fusion = f32[320]{0:T(512)S(1)} fusion(bf16[320,8192]{1,0:T(8,128)(2,1)} %all-reduce.2.cloned.1.call-done, bf16[320,8192]{1,0:T(8,128)(2,1)} %param.13), kind=kLoop, calls=%fused_computation.13 | loop fusion | flops 13106880 | bytes 10487040 | tf_op jit(solution)/shard_map/reduce_sum | solution.py:106
  325.1 0.0 copy-done.2
  325.1 7.1 %multiply_convert_fusion = bf16[320,8192]{1,0:T(8,128)(2,1)} fusion(bf16[320,8192]{1,0:T(8,128)(2,1)S(1)} %copy-done.2, bf16[320,8192]{1,0:T(8,128)(2,1)} %param.13, f32[8192]{0:T(1024)S(1)} %convert_element_type.52, f32[320]{0:T(512)S(1)} %add_rsqrt_fusion), kind=kLoop, calls=%fused_computation.12 | loop fusion | flops 15728640 | bytes 15762688 | tf_op jit(solution)/shard_map/convert_element_type | solution.py:107
  332.2 0.0 copy-done.1
  (15 shorter events, 0.2 us)
Async XLA Ops:
  7.2 145.7 %copy-start = (bf16[320,512]{1,0:T(8,128)(2,1)S(1)}, bf16[320,512]{1,0:T(8,128)(2,1)}, u32[]{:S(2)}) copy-start(bf16[320,512]{1,0:T(8,128)(2,1)} %param.9) | copy-start | bytes 983044
  7.2 16.7 %copy-start.4 = (s32[18]{0:T(128)S(1)}, s32[18]{0:T(128)}, u32[]{:S(2)}) copy-start(s32[18]{0:T(128)} %param.15) | copy-start | bytes 220
  7.2 17.0 %copy-start.3 = (bf16[8192]{0:T(1024)(128)(2,1)S(1)}, bf16[8192]{0:T(1024)(128)(2,1)}, u32[]{:S(2)}) copy-start(bf16[8192]{0:T(1024)(128)(2,1)} %param.14) | copy-start | bytes 49156
  11.1 141.7 %all-to-all-start = ((bf16[32,320,256]{2,1,0:T(8,128)(2,1)}), bf16[32,320,256]{2,1,0:T(8,128)(2,1)}, u32[]{:S(2)}, u32[]{:S(2)}) async-start(bf16[32,320,256]{2,1,0:T(8,128)(2,1)} %stack.2), calls=%async_computation | async-start | bytes 10485760 | tf_op jit(solution)/shard_map/all_to_all | solution.py:68
  23.1 199.4 %all-gather.2.cloned.1.call-start = ((), (), s32[]{:S(2)}) async-start(), calls=%async_computation.1 | async-start | bytes 8650752 | tf_op jit(solution)/shard_map/all_gather | solution.py:101
  23.9 295.2 %all-reduce.2.cloned.1.call-start = ((), (), s32[]{:S(2)}) async-start(), calls=%async_computation.2 | async-start | bytes 10485760 | tf_op jit(solution)/shard_map/psum | solution.py:104
  319.1 6.0 %copy-start.2 = (bf16[320,8192]{1,0:T(8,128)(2,1)S(1)}, bf16[320,8192]{1,0:T(8,128)(2,1)}, u32[]{:S(2)}) copy-start(bf16[320,8192]{1,0:T(8,128)(2,1)} %all-reduce.2.cloned.1.call-done) | copy-start | bytes 15728644
  319.1 13.1 %copy-start.1 = (bf16[320,512]{1,0:T(8,128)(2,1)S(1)}, bf16[320,512]{1,0:T(8,128)(2,1)}, u32[]{:S(2)}) copy-start(bf16[320,512]{1,0:T(8,128)(2,1)} %param.9) | copy-start | bytes 983044
Sparse Core Ops, SparseCore 0:
  26.4 169.8 all-gather.1
  230.9 88.2 all-reduce.1
